TPU v7x, 32 devices: a whole 2x2x4 slice. The times are simulated.
32 devices in a mesh: expert: 8 (over z, x), tensor: 4 (over y, core).
Axes of the slice: x: 2, y: 2, z: 4, core: 2. Of those that a mesh axis runs over, the one named last changes fastest.
Arguments:
- attn_heads: bfloat16 [1024, 4096], P('expert', 'tensor'), may hold values from -6 to 6
- out_proj: bfloat16 [4096, 4096], P('tensor', 'expert'), may hold values from -0.09375 to 0.09375
- residual: bfloat16 [1024, 4096], P('expert'), may hold values from -6 to 6
- norm_gain: bfloat16 [4096], replicated, may hold values from 0.099609375 to 1.8984375
- gate_proj: bfloat16 [16, 1536, 4096], P('expert', 'tensor'), may hold values from -0.09375 to 0.09375
- up_proj: bfloat16 [16, 1536, 4096], P('expert', 'tensor'), may hold values from -0.09375 to 0.09375
- down_proj: bfloat16 [16, 1536, 4096], P('expert', None, 'tensor'), may hold values from -0.15625 to 0.15625
- expert_ids: int32 [1024, 8], P('expert'), may hold values from 0 to 15, all different within a row; in each aligned block of 128 rows (0 to 127, 128 to 255, ...) at most 96 rows name the same one
- gate_scores: float32 [1024, 8], P('expert'), may hold values from 0.25 to 1
Outputs:
- layer_out: bfloat16 [1024, 4096], P('expert', 'tensor')
Inputs may be any that keep to these rules, and one draw needn't show every extreme that they name: `expert_ids`: each row names 8 different experts. Among the 128 rows of one device no expert is named by more than 96 rows, a bound that some block reaches.
All inputs are finite; a program needn't handle non-finite values.
Results may differ from a plain program's by a relative error of at most 0.0051.
Values may be sent and summed in bfloat16 or wider, within the bound.
No kernel may reach another device: no remote copies, remote signals or barrier semaphores. Data moves between devices by JAX's collectives and lax.ppermute only.
A program may use at most 128 MiB of HBM per device.

v0:
```python
import jax
import jax.numpy as jnp
from jax import lax
from jax.sharding import PartitionSpec as P

EPS = 1e-06


def on_device(
    attn_heads,
    out_proj,
    residual,
    norm_gain,
    gate_proj,
    up_proj,
    down_proj,
    expert_ids,
    gate_scores,
):
    tok_count = residual.shape[0]
    width = residual.shape[1]
    topk = expert_ids.shape[1]
    groups = lax.axis_size("expert")
    tensor_ways = lax.axis_size("tensor")
    exp_local = gate_proj.shape[0]
    experts_all = groups * exp_local
    slot_cap = 3 * tok_count * topk // (2 * experts_all)
    share = width // tensor_ways
    offset = lax.axis_index("tensor") * share
    partial_proj = jnp.dot(
        attn_heads,
        lax.all_gather(out_proj, "expert", axis=1, tiled=True),
        preferred_element_type=jnp.float32,
    )
    attn_part = lax.psum_scatter(partial_proj, "tensor", scatter_dimension=1, tiled=True)
    res_part = lax.dynamic_slice_in_dim(residual, offset, share, 1)
    state_part = (res_part.astype(jnp.float32) + attn_part).astype(jnp.bfloat16)
    state_f = state_part.astype(jnp.float32)
    squares = lax.psum(jnp.sum(state_f * state_f, axis=1), "tensor")
    gain_part = lax.dynamic_slice_in_dim(norm_gain, offset, share, 0)
    normed = (
        state_f * lax.rsqrt(squares / width + EPS)[:, None] * gain_part.astype(jnp.float32)
    ).astype(jnp.bfloat16)
    picks = expert_ids[:, :, None] == jnp.arange(experts_all, dtype=jnp.int32)[None, None, :]
    flag = jnp.sum(picks.astype(jnp.int32), axis=1)
    before = jnp.cumsum(flag, axis=0) - flag
    rank = jnp.sum(jnp.where(picks, before[:, None, :], 0), axis=2)
    slot = expert_ids * slot_cap + rank
    token_ids = jnp.arange(tok_count * topk, dtype=jnp.int32) // topk + 1
    owner = jnp.zeros((experts_all * slot_cap,), jnp.int32).at[slot.reshape(-1)].set(token_ids)
    rows = jnp.take(normed, jnp.maximum(owner - 1, 0), axis=0)
    rows = jnp.where((owner > 0)[:, None], rows, jnp.zeros((), jnp.bfloat16))
    send = rows.reshape(groups, exp_local, slot_cap, rows.shape[1])
    block = lax.all_gather(
        lax.all_to_all(send, "expert", split_axis=0, concat_axis=0, tiled=True),
        "tensor",
        axis=3,
        tiled=True,
    )
    count = block.shape[2]
    stacked = jnp.transpose(block, (1, 0, 2, 3)).reshape(exp_local, groups * count, width)
    gate = jnp.einsum("erd,efd->erf", stacked, gate_proj, preferred_element_type=jnp.float32)
    upper = jnp.einsum("erd,efd->erf", stacked, up_proj, preferred_element_type=jnp.float32)
    act = (jax.nn.silu(gate) * upper).astype(jnp.bfloat16)
    whole_act = lax.all_gather(act, "tensor", axis=2, tiled=True)
    result = jnp.einsum(
        "erf,efd->erd", whole_act, down_proj, preferred_element_type=jnp.float32
    ).astype(jnp.bfloat16)
    result = jnp.transpose(result.reshape(exp_local, groups, count, share), (1, 0, 2, 3))
    back = lax.all_to_all(result, "expert", split_axis=0, concat_axis=0, tiled=True)
    flat = back.reshape(experts_all * slot_cap, share)
    picked = jnp.take(flat, slot.reshape(-1), axis=0).reshape(tok_count, topk, share)
    weights = gate_scores / jnp.sum(gate_scores, axis=1, keepdims=True)
    mixture = jnp.einsum("tk,tkd->td", weights, picked.astype(jnp.float32))
    return (state_part.astype(jnp.float32) + mixture).astype(jnp.bfloat16)


def solution(mesh):
    in_specs = (
        P("expert", "tensor"),
        P("tensor", "expert"),
        P("expert", None),
        P(),
        P("expert", "tensor", None),
        P("expert", "tensor", None),
        P("expert", None, "tensor"),
        P("expert", None),
        P("expert", None),
    )
    out_specs = P("expert", "tensor")
    return jax.shard_map(
        on_device, mesh=mesh, in_specs=in_specs, out_specs=out_specs, check_vma=False
    )
```

profile of v0, /device:TPU:0, one launch (start us, length us, event | category | flops | bytes accessed | tf_op | source)
XLA Modules:
  0.0 507.4 jit_solution(3773535396827234200)
XLA Ops:
  6.5 0.0 copy-start
  6.5 0.0 all-gather.4.cloned.1.call-start
  6.5 0.7 all-gather.4.cloned.1.call-update
  7.3 0.0 copy-start.4
  7.3 0.0 reduce-scatter.2.cloned.1.call-start
  7.3 130.2 %all-gather.4.cloned.1.call-done = bf16[1024,4096]{1,0:T(8,128)(2,1)} async-done(((bf16[1024,512]{1,0:T(8,128)(2,1)}), bf16[1024,4096]{1,0:T(8,128)(2,1)}) %all-gather.4.cloned.1.call-update) | async-done | bytes 8388624 | tf_op jit(solution)/shard_map/all_gather | solution.py:32
  137.5 0.0 copy-done
  137.5 6.0 %fusion.14 = f32[128,4096]{1,0:T(8,128)} fusion(bf16[128,1024]{1,0:T(8,128)(2,1)S(1)} %copy-done, bf16[1024,4096]{1,0:T(8,128)(2,1)} %all-gather.4.cloned.1.call-done), kind=kOutput, calls=%fused_computation.45 | convolution fusion | flops 1073741824 | bytes 10747904 | tf_op jit(solution)/shard_map/dot_general | solution.py:30
  143.5 0.0 reduce-scatter.2.cloned.1.call-update
  143.5 0.0 all-gather.6.cloned.1.call-start
  143.6 0.0 copy-done.4
  143.6 0.1 copy.26
  143.7 0.2 reduce_window_sum.11
  143.9 0.1 copy.28
  144.0 0.1 copy.30
  144.1 0.1 reshape.84
  144.3 4.3 scatter_custom_fusion
  148.6 0.1 broadcast_in_dim.61
  148.7 0.1 broadcast_in_dim.63
  148.8 0.7 dynamic-slice_convert_fusion
  149.5 23.8 %reduce-scatter.2.cloned.1.call-done = f32[128,1024]{1,0:T(8,128)} async-done(((f32[128,4096]{1,0:T(8,128)}), f32[128,1024]{1,0:T(8,128)}) %reduce-scatter.2.cloned.1.call-update) | async-done | bytes 524304 | tf_op jit(solution)/shard_map/reduce_scatter | solution.py:35
  173.3 1.3 fusion.3
  174.6 0.0 copy-start.2
  174.6 5.8 %psum.7 = f32[128]{0:T(128)S(1)} all-reduce(f32[128]{0:T(128)S(1)} %get-tuple-element.7), channel_id=1, replica_groups=mesh['expert'=8,'tensor'=4] {'tensor'}, use_global_device_ids=true, to_apply=%region_7.8 | all-reduce | flops 128 | bytes 1024 | tf_op jit(solution)/shard_map/psum | solution.py:39
  180.3 0.0 copy-done.2
  180.4 0.1 fusion.5
  180.5 5.1 gather_fusion
  185.6 0.6 select_select_fusion
  186.2 76.2 %all_to_all.10 = bf16[8,2,96,1024]{3,2,1,0:T(8,128)(2,1)} all-to-all(bf16[8,2,96,1024]{3,2,1,0:T(8,128)(2,1)S(1)} %select_select_fusion), channel_id=1, replica_groups=mesh['expert'=8,'tensor'=4] {'expert'}, dimensions={0} | all-to-all | bytes 6291456 | tf_op jit(solution)/shard_map/all_to_all | solution.py:55
  262.4 0.0 slice-start
  262.4 0.0 all-gather.6.cloned.1.call-update
  262.5 0.2 all-gather.8.cloned.1.call-start
  262.7 80.0 %all-gather.6.cloned.1.call-done = bf16[8,2,96,4096]{3,2,1,0:T(8,128)(2,1)} async-done(((bf16[8,2,96,1024]{3,2,1,0:T(8,128)(2,1)}), bf16[8,2,96,4096]{3,2,1,0:T(8,128)(2,1)}) %all-gather.6.cloned.1.call-update) | async-done | bytes 12582928 | tf_op jit(solution)/shard_map/all_gather | solution.py:54
  342.7 0.0 slice-start.1
  342.7 6.6 %copy.31 = bf16[2,8,96,4096]{3,2,1,0:T(8,128)(2,1)S(1)} copy(bf16[2,8,96,4096]{3,2,0,1:T(8,128)(2,1)} %bitcast.26) | data formatting | bytes 25165824 | tf_op jit(solution)/shard_map/transpose | solution.py:61
  349.3 0.0 slice-done
  349.3 0.0 slice-done.1
  349.3 8.1 %fusion.15 = f32[2,768,384]{2,1,0:T(8,128)} fusion(bf16[2,768,4096]{2,1,0:T(8,128)(2,1)S(1)} %bitcast.27, bf16[2,384,4096]{2,1,0:T(8,128)(2,1)S(1)} %bitcast.35), kind=kOutput, calls=%fused_computation.46 | convolution fusion | flops 4831838208 | bytes 21233664 | tf_op jit(solution)/shard_map/erd,efd->erf/dot_general | solution.py:62
  357.4 10.0 %multiply_convert_fusion = bf16[2,768,384]{2,1,0:T(8,128)(2,1)} fusion(f32[2,768,384]{2,1,0:T(8,128)} %fusion.15, bf16[2,768,4096]{2,1,0:T(8,128)(2,1)S(1)} %bitcast.28, bf16[2,384,4096]{2,1,0:T(8,128)(2,1)} %param.14), kind=kOutput, calls=%fused_computation.5 | convolution fusion | flops 4835377152 | bytes 22413312 | tf_op jit(solution)/shard_map/erd,efd->erf/dot_general | solution.py:63
  367.4 0.0 all-gather.8.cloned.1.call-update
  367.5 37.6 %all-gather.8.cloned.1.call-done = bf16[2,768,1536]{2,1,0:T(8,128)(2,1)} async-done(((bf16[2,768,384]{2,1,0:T(8,128)(2,1)}), bf16[2,768,1536]{2,1,0:T(8,128)(2,1)}) %all-gather.8.cloned.1.call-update) | async-done | bytes 4718608 | tf_op jit(solution)/shard_map/all_gather | solution.py:65
  405.0 8.6 %convolution_convert_fusion = bf16[2,768,1024]{2,1,0:T(8,128)(2,1)S(1)} fusion(bf16[2,768,1536]{2,1,0:T(8,128)(2,1)} %all-gather.8.cloned.1.call-done, bf16[2,1536,1024]{2,1,0:T(8,128)(2,1)} %param.15), kind=kOutput, calls=%fused_computation.6 | convolution fusion | flops 4833411072 | bytes 14155776 | tf_op jit(solution)/shard_map/erf,efd->erd/dot_general | solution.py:66
  413.6 1.9 copy.37
  415.5 0.0 copy-start.5
  415.5 5.6 %all-to-all-start.1 = ((bf16[8,2,96,1024]{3,2,1,0:T(8,128)(2,1)}), bf16[8,2,96,1024]{3,2,1,0:T(8,128)(2,1)S(1)}, u32[]{:S(2)}, u32[]{:S(2)}) async-start(bf16[8,2,96,1024]{3,2,1,0:T(8,128)(2,1)} %bitcast.29), calls=%async_computation.2 | async-start | bytes 6291456 | tf_op jit(solution)/shard_map/all_to_all | solution.py:70
  421.2 0.1 copy.29
  421.3 0.0 copy-done.5
  421.3 0.1 copy.33
  421.5 70.8 %all-to-all-done.1 = bf16[8,2,96,1024]{3,2,1,0:T(8,128)(2,1)S(1)} async-done(((bf16[8,2,96,1024]{3,2,1,0:T(8,128)(2,1)}), bf16[8,2,96,1024]{3,2,1,0:T(8,128)(2,1)S(1)}, u32[]{:S(2)}, u32[]{:S(2)}) %all-to-all-start.1) | async-done | bytes 3145760 | tf_op jit(solution)/shard_map/all_to_all | solution.py:70
  492.3 0.0 copy-start.1
  492.3 5.3 %gather_fusion.1 = bf16[1024,1024]{1,0:T(8,128)(2,1)} fusion(bf16[1536,1024]{1,0:T(8,128)(2,1)S(1)} %bitcast.25, s32[1024]{0:T(1024)S(1)} %broadcast_clamp_fusion), kind=kCustom, calls=%fused_computation.1 | custom fusion | bytes 4198400 | tf_op jit(solution)/shard_map/jit(_take)/gather | solution.py:72
  497.6 0.0 copy-start.3
  497.6 2.4 fusion
  500.1 0.0 copy-done.3
  500.1 0.8 fusion.6
  500.9 0.0 copy-done.1
  (14 shorter events, 0.1 us)
Async XLA Ops:
  6.5 131.0 %copy-start = (bf16[128,1024]{1,0:T(8,128)(2,1)S(1)}, bf16[128,1024]{1,0:T(8,128)(2,1)}, u32[]{:S(2)}) copy-start(bf16[128,1024]{1,0:T(8,128)(2,1)} %param.9) | copy-start | bytes 786436
  6.5 131.0 %all-gather.4.cloned.1.call-start = ((), (), s32[]{:S(2)}) async-start(), calls=%async_computation.3 | async-start | bytes 9437184 | tf_op jit(solution)/shard_map/all_gather | solution.py:32
  7.3 136.3 %copy-start.4 = (s32[128,8]{0,1:T(8,128)S(1)}, s32[128,8]{0,1:T(8,128)}, u32[]{:S(2)}) copy-start(s32[128,8]{0,1:T(8,128)} %param.16) | copy-start | bytes 12292
  7.3 166.0 %reduce-scatter.2.cloned.1.call-start = ((), (), s32[]{:S(2)}) async-start(), calls=%async_computation.4 | async-start | bytes 2621440 | tf_op jit(solution)/shard_map/reduce_scatter | solution.py:35
  143.5 199.1 %all-gather.6.cloned.1.call-start = ((), (), s32[]{:S(2)}) async-start(), calls=%async_computation.5 | async-start | bytes 15728640 | tf_op jit(solution)/shard_map/all_gather | solution.py:54
  174.6 5.8 %copy-start.2 = (bf16[128,1024]{1,0:T(8,128)(2,1)}, bf16[128,1024]{1,0:T(8,128)(2,1)S(1)}, u32[]{:S(2)}) copy-start(bf16[128,1024]{1,0:T(8,128)(2,1)S(1)} %get-tuple-element.8) | copy-start | bytes 786436
  262.4 86.8 %slice-start = ((s8[6291456]{0:T(1024)(128)(4,1)}), s8[2097152]{0:T(1024)(128)(4,1)S(1)}, s32[]{:S(2)}) async-start(s8[6291456]{0:T(1024)(128)(4,1)} %bitcast.34), calls=%async_computation.7 | async-start | bytes 4194304
  262.5 142.5 %all-gather.8.cloned.1.call-start = ((), (), s32[]{:S(2)}) async-start(), calls=%async_computation.6 | async-start | bytes 5898240 | tf_op jit(solution)/shard_map/all_gather | solution.py:65
  342.7 6.6 %slice-start.1 = ((s8[6291456]{0:T(1024)(128)(4,1)}), s8[4194304]{0:T(1024)(128)(4,1)S(1)}, s32[]{:S(2)}) async-start(s8[6291456]{0:T(1024)(128)(4,1)} %bitcast.34), calls=%async_computation.8 | async-start | bytes 8388608
  415.5 5.8 %copy-start.5 = (f32[128,8]{0,1:T(8,128)S(1)}, f32[128,8]{0,1:T(8,128)}, u32[]{:S(2)}) copy-start(f32[128,8]{0,1:T(8,128)} %param.17) | copy-start | bytes 12292
  415.5 76.8 %all-to-all-start.1 = ((bf16[8,2,96,1024]{3,2,1,0:T(8,128)(2,1)}), bf16[8,2,96,1024]{3,2,1,0:T(8,128)(2,1)S(1)}, u32[]{:S(2)}, u32[]{:S(2)}) async-start(bf16[8,2,96,1024]{3,2,1,0:T(8,128)(2,1)} %bitcast.29), calls=%async_computation.2 | async-start | bytes 6291456 | tf_op jit(solution)/shard_map/all_to_all | solution.py:70
  492.3 8.6 %copy-start.1 = (bf16[128,1024]{1,0:T(8,128)(2,1)S(1)}, bf16[128,1024]{1,0:T(8,128)(2,1)}, u32[]{:S(2)}) copy-start(bf16[128,1024]{1,0:T(8,128)(2,1)} %param.9) | copy-start | bytes 786436
  497.6 2.4 copy-start.3
Sparse Core Ops, SparseCore 0:
  9.4 128.0 all-gather.3
  143.7 29.5 reduce-scatter.1
  262.6 80.0 all-gather.5
  367.6 37.3 all-gather.7
where the time goes:
time: 508 us; the launch traced here: 507 us
  waiting for transfers between devices  343 us (68%)
  blocking collectives  82 us (16%)
  matrix products  35.1 us (7%)
  local copies, waits for them, and re-layouts  24.1 us (5%)
  between operations  13.3 us (3%)
  starting transfers between devices  5.95 us (1%)
    all_gather x1, waiting for transfers between devices, on_device(): lax.all_gather(out_proj, 'expert', axis=1, tiled=True)  130 us
    all_gather x1, waiting for transfers between devices, on_device(): lax.all_gather(lax.all_to_all(send, 'expert', split_axis=0, concat_axis=0...  80 us
    all_to_all x1, blocking collectives, on_device(): lax.all_to_all(send, 'expert', split_axis=0, concat_axis=0, tiled=True)  76.2 us
    all_to_all x1, waiting for transfers between devices, on_device(): lax.all_to_all(result, 'expert', split_axis=0, concat_axis=0, tiled=True)  70.8 us
    all_gather x1, waiting for transfers between devices, on_device(): whole_act = lax.all_gather(act, 'tensor', axis=2, tiled=True)  37.6 us
    reduce_scatter x1, waiting for transfers between devices, on_device(): lax.psum_scatter(partial_proj, 'tensor', scatter_dimension=1, tiled=True)  23.8 us
  transfers between devices with their start and end apart: 5, of which 5 were waited for; matrix products, arithmetic and copies ran while one was open for 1% of the time, Pallas kernels for 0%

commit v1 on v0

--- a/solution.py
+++ b/solution.py
@@ -62,9 +62,38 @@
     gate = jnp.einsum("erd,efd->erf", stacked, gate_proj, preferred_element_type=jnp.float32)
     upper = jnp.einsum("erd,efd->erf", stacked, up_proj, preferred_element_type=jnp.float32)
     act = (jax.nn.silu(gate) * upper).astype(jnp.bfloat16)
-    whole_act = lax.all_gather(act, "tensor", axis=2, tiled=True)
-    result = jnp.einsum(
-        "erf,efd->erd", whole_act, down_proj, preferred_element_type=jnp.float32
+
+    def _register_shapes(local_x, unit):
+        made = []
+        v_now, value_now, block_now = (
+            lax.axis_size("tensor"),
+            lax.axis_index("tensor"),
+            local_x.shape[2],
+        )
+        for i in range(v_now):
+            made.append((i, (i + 1) % v_now))
+        crops = []
+        for i in range(v_now):
+            crops.append((i, (i - 1) % v_now))
+        y2 = v_now // 2
+        u1 = inter = local_x
+        next_value = unit(local_x, value_now * block_now)
+        for pp in range(1, y2 + 1):
+            u1 = lax.ppermute(u1, axis_name="tensor", perm=made)
+            if pp < v_now - y2:
+                inter = lax.ppermute(inter, axis_name="tensor", perm=crops)
+                next_value = next_value + unit(inter, (value_now + pp) % v_now * block_now)
+            next_value = next_value + unit(u1, (value_now - pp) % v_now * block_now)
+        return next_value
+
+    result = _register_shapes(
+        act,
+        lambda part, offset_2: jnp.einsum(
+            "erf,efd->erd",
+            part,
+            lax.dynamic_slice_in_dim(down_proj, offset_2, part.shape[2], axis=1),
+            preferred_element_type=jnp.float32,
+        ),
     ).astype(jnp.bfloat16)
     result = jnp.transpose(result.reshape(exp_local, groups, count, share), (1, 0, 2, 3))
     back = lax.all_to_all(result, "expert", split_axis=0, concat_axis=0, tiled=True)

time: 508 us -> 505 us (level)
  waiting for transfers between devices: 343 us -> 334 us
    all_gather x1 -> x0, waiting for transfers between devices: 37.6 us -> none  [on_device(): whole_act = lax.all_gather(act, 'tensor', axis=2, tiled=True)]
    ppermute x0 -> x3, waiting for transfers between devices: none -> 31.7 us  [the longest x2 31.7 us: _register_shapes(): u1 = lax.ppermute(u1, axis_name='tensor', perm=made)]
    dot_general x1 -> x4, matrix products: 8.55 us -> 13.8 us  [on_device(): jnp.einsum('erf,efd->erd', part, lax.dynamic_slice_in_dim(down_proj, offs...]
  transfers between devices with their start and end apart: 5 -> 7, of which waited for: 5 -> 6; matrix products, arithmetic and copies ran while one was open for 1% -> 3% of each run, Pallas kernels for 0% -> 0%
where the time goes in v1:
time: 505 us; the launch traced here: 504 us
  waiting for transfers between devices  334 us (66%)
  blocking collectives  82 us (16%)
  matrix products  39.4 us (8%)
  local copies, waits for them, and re-layouts  24.1 us (5%)
  between operations  13.3 us (3%)
  starting transfers between devices  7.29 us (1%)
    all_gather x1, waiting for transfers between devices, on_device(): lax.all_gather(out_proj, 'expert', axis=1, tiled=True)  130 us
    all_gather x1, waiting for transfers between devices, on_device(): lax.all_gather(lax.all_to_all(send, 'expert', split_axis=0, concat_axis=0...  80.2 us
    all_to_all x1, blocking collectives, on_device(): lax.all_to_all(send, 'expert', split_axis=0, concat_axis=0, tiled=True)  76.2 us
    all_to_all x1, waiting for transfers between devices, on_device(): lax.all_to_all(result, 'expert', split_axis=0, concat_axis=0, tiled=True)  67.6 us
    ppermute x2, waiting for transfers between devices, _register_shapes(): u1 = lax.ppermute(u1, axis_name='tensor', perm=made)  31.7 us
    reduce_scatter x1, waiting for transfers between devices, on_device(): lax.psum_scatter(partial_proj, 'tensor', scatter_dimension=1, tiled=True)  23.8 us
    dot_general x4, matrix products, on_device(): jnp.einsum('erf,efd->erd', part, lax.dynamic_slice_in_dim(down_proj, offs...  13.8 us
  transfers between devices with their start and end apart: 7, of which 6 were waited for; matrix products, arithmetic and copies ran while one was open for 3% of the time, Pallas kernels for 0%

profile of v1, /device:TPU:0, one launch (start us, length us, event | category | flops | bytes accessed | tf_op | source)
XLA Modules:
  0.0 504.3 jit_solution(9716785739695626151)
XLA Ops:
  6.5 0.0 copy-start
  6.5 0.0 all-gather.3.cloned.1.call-start
  6.5 0.7 all-gather.3.cloned.1.call-update
  7.3 0.0 copy-start.4
  7.3 0.0 reduce-scatter.2.cloned.1.call-start
  7.3 130.2 %all-gather.3.cloned.1.call-done = bf16[1024,4096]{1,0:T(8,128)(2,1)} async-done(((bf16[1024,512]{1,0:T(8,128)(2,1)}), bf16[1024,4096]{1,0:T(8,128)(2,1)}) %all-gather.3.cloned.1.call-update) | async-done | bytes 8388624 | tf_op jit(solution)/shard_map/all_gather | solution.py:32
  137.5 0.0 copy-done
  137.5 6.0 %fusion.25 = f32[128,4096]{1,0:T(8,128)} fusion(bf16[128,1024]{1,0:T(8,128)(2,1)S(1)} %copy-done, bf16[1024,4096]{1,0:T(8,128)(2,1)} %all-gather.3.cloned.1.call-done), kind=kOutput, calls=%fused_computation.56 | convolution fusion | flops 1073741824 | bytes 10747904 | tf_op jit(solution)/shard_map/dot_general | solution.py:30
  143.5 0.0 reduce-scatter.2.cloned.1.call-update
  143.5 0.0 all-gather.5.cloned.1.call-start
  143.6 0.0 copy-done.4
  143.6 0.1 copy.26
  143.7 0.2 reduce_window_sum.11
  143.9 0.1 copy.28
  144.0 0.1 copy.30
  144.1 0.1 reshape.84
  144.3 4.3 scatter_custom_fusion
  148.6 0.1 broadcast_in_dim.61
  148.7 0.1 broadcast_in_dim.63
  148.8 0.7 dynamic-slice_convert_fusion
  149.5 23.8 %reduce-scatter.2.cloned.1.call-done = f32[128,1024]{1,0:T(8,128)} async-done(((f32[128,4096]{1,0:T(8,128)}), f32[128,1024]{1,0:T(8,128)}) %reduce-scatter.2.cloned.1.call-update) | async-done | bytes 524304 | tf_op jit(solution)/shard_map/reduce_scatter | solution.py:35
  173.3 1.3 fusion.10
  174.6 0.0 copy-start.2
  174.6 5.8 %psum.7 = f32[128]{0:T(128)S(1)} all-reduce(f32[128]{0:T(128)S(1)} %get-tuple-element.7), channel_id=1, replica_groups=mesh['expert'=8,'tensor'=4] {'tensor'}, use_global_device_ids=true, to_apply=%region_7.8 | all-reduce | flops 128 | bytes 1024 | tf_op jit(solution)/shard_map/psum | solution.py:39
  180.3 0.0 copy-done.2
  180.4 0.1 fusion.12
  180.5 5.1 %gather_fusion = bf16[1536,1024]{1,0:T(8,128)(2,1)S(1)} fusion(bf16[128,1024]{1,0:T(8,128)(2,1)S(1)} %fusion.12, s32[2048]{0:T(1024)S(1)} %pad_clamp_fusion), kind=kCustom, calls=%fused_computation | custom fusion | bytes 6297600 | tf_op jit(solution)/shard_map/jit(_take)/gather | solution.py:51
  185.6 0.6 select_select_fusion
  186.2 76.2 %all_to_all.10 = bf16[8,2,96,1024]{3,2,1,0:T(8,128)(2,1)} all-to-all(bf16[8,2,96,1024]{3,2,1,0:T(8,128)(2,1)S(1)} %select_select_fusion), channel_id=1, replica_groups=mesh['expert'=8,'tensor'=4] {'expert'}, dimensions={0} | all-to-all | bytes 6291456 | tf_op jit(solution)/shard_map/all_to_all | solution.py:55
  262.4 0.0 slice-start
  262.4 0.0 all-gather.5.cloned.1.call-update
  262.5 80.2 %all-gather.5.cloned.1.call-done = bf16[8,2,96,4096]{3,2,1,0:T(8,128)(2,1)} async-done(((bf16[8,2,96,1024]{3,2,1,0:T(8,128)(2,1)}), bf16[8,2,96,4096]{3,2,1,0:T(8,128)(2,1)}) %all-gather.5.cloned.1.call-update) | async-done | bytes 12582928 | tf_op jit(solution)/shard_map/all_gather | solution.py:54
  342.7 0.0 slice-start.1
  342.7 6.6 %copy.31 = bf16[2,8,96,4096]{3,2,1,0:T(8,128)(2,1)S(1)} copy(bf16[2,8,96,4096]{3,2,0,1:T(8,128)(2,1)} %bitcast.28) | data formatting | bytes 25165824 | tf_op jit(solution)/shard_map/transpose | solution.py:61
  349.3 0.0 slice-done
  349.3 0.0 slice-done.1
  349.3 8.1 %fusion.26 = f32[2,768,384]{2,1,0:T(8,128)} fusion(bf16[2,768,4096]{2,1,0:T(8,128)(2,1)S(1)} %bitcast.29, bf16[2,384,4096]{2,1,0:T(8,128)(2,1)S(1)} %bitcast.37), kind=kOutput, calls=%fused_computation.57 | convolution fusion | flops 4831838208 | bytes 21233664 | tf_op jit(solution)/shard_map/erd,efd->erf/dot_general | solution.py:62
  357.4 9.2 %multiply_convert_fusion = bf16[2,768,384]{2,1,0:T(8,128)(2,1)S(1)} fusion(f32[2,768,384]{2,1,0:T(8,128)} %fusion.26, bf16[2,768,4096]{2,1,0:T(8,128)(2,1)S(1)} %bitcast.30, bf16[2,384,4096]{2,1,0:T(8,128)(2,1)} %param.14), kind=kOutput, calls=%fused_computation.6 | convolution fusion | flops 4835377152 | bytes 22413312 | tf_op jit(solution)/shard_map/erd,efd->erf/dot_general | solution.py:63
  366.6 0.3 collective-permute-start.1
  366.9 1.5 collective-permute-start
  368.4 26.0 %collective-permute-done.1 = bf16[2,768,384]{2,1,0:T(8,128)(2,1)S(1)} collective-permute-done((bf16[2,768,384]{2,1,0:T(8,128)(2,1)S(1)}, bf16[2,768,384]{2,1,0:T(8,128)(2,1)S(1)}, u32[]{:S(2)}, u32[]{:S(2)}) %collective-permute-start.1) | collective-permute-done | bytes 1179680 | tf_op jit(solution)/shard_map/ppermute | solution.py:82
  394.3 0.0 collective-permute-start.2
  394.3 3.2 fusion.7
  397.5 3.2 fusion.3
  400.8 0.0 collective-permute-done
  400.8 3.6 fusion.5
  404.3 5.7 %collective-permute-done.2 = bf16[2,768,384]{2,1,0:T(8,128)(2,1)} collective-permute-done((bf16[2,768,384]{2,1,0:T(8,128)(2,1)S(1)}, bf16[2,768,384]{2,1,0:T(8,128)(2,1)}, u32[]{:S(2)}, u32[]{:S(2)}) %collective-permute-start.2) | collective-permute-done | bytes 1179680 | tf_op jit(solution)/shard_map/ppermute | solution.py:82
  410.1 3.8 add_convert_fusion
  413.9 2.0 copy.37
  415.9 0.0 copy-start.5
  415.9 5.4 %all-to-all-start.1 = ((bf16[8,2,96,1024]{3,2,1,0:T(8,128)(2,1)}), bf16[8,2,96,1024]{3,2,1,0:T(8,128)(2,1)S(1)}, u32[]{:S(2)}, u32[]{:S(2)}) async-start(bf16[8,2,96,1024]{3,2,1,0:T(8,128)(2,1)} %bitcast.31), calls=%async_computation.2 | async-start | bytes 6291456 | tf_op jit(solution)/shard_map/all_to_all | solution.py:99
  421.3 0.1 copy.29
  421.4 0.0 copy-done.5
  421.4 0.1 copy.33
  421.6 67.6 %all-to-all-done.1 = bf16[8,2,96,1024]{3,2,1,0:T(8,128)(2,1)S(1)} async-done(((bf16[8,2,96,1024]{3,2,1,0:T(8,128)(2,1)}), bf16[8,2,96,1024]{3,2,1,0:T(8,128)(2,1)S(1)}, u32[]{:S(2)}, u32[]{:S(2)}) %all-to-all-start.1) | async-done | bytes 3145760 | tf_op jit(solution)/shard_map/all_to_all | solution.py:99
  489.2 0.0 copy-start.1
  489.2 5.3 %gather_fusion.1 = bf16[1024,1024]{1,0:T(8,128)(2,1)} fusion(bf16[1536,1024]{1,0:T(8,128)(2,1)S(1)} %bitcast.27, s32[1024]{0:T(1024)S(1)} %broadcast_clamp_fusion), kind=kCustom, calls=%fused_computation.1 | custom fusion | bytes 4198400 | tf_op jit(solution)/shard_map/jit(_take)/gather | solution.py:101
  494.5 0.0 copy-start.3
  494.5 2.4 fusion
  497.0 0.0 copy-done.3
  497.0 0.8 fusion.13
  497.8 0.0 copy-done.1
  (14 shorter events, 0.1 us)
Async XLA Ops:
  6.5 131.0 %copy-start = (bf16[128,1024]{1,0:T(8,128)(2,1)S(1)}, bf16[128,1024]{1,0:T(8,128)(2,1)}, u32[]{:S(2)}) copy-start(bf16[128,1024]{1,0:T(8,128)(2,1)} %param.9) | copy-start | bytes 786436
  6.5 131.0 %all-gather.3.cloned.1.call-start = ((), (), s32[]{:S(2)}) async-start(), calls=%async_computation.3 | async-start | bytes 9437184 | tf_op jit(solution)/shard_map/all_gather | solution.py:32
  7.3 136.3 %copy-start.4 = (s32[128,8]{0,1:T(8,128)S(1)}, s32[128,8]{0,1:T(8,128)}, u32[]{:S(2)}) copy-start(s32[128,8]{0,1:T(8,128)} %param.16) | copy-start | bytes 12292
  7.3 166.0 %reduce-scatter.2.cloned.1.call-start = ((), (), s32[]{:S(2)}) async-start(), calls=%async_computation.4 | async-start | bytes 2621440 | tf_op jit(solution)/shard_map/reduce_scatter | solution.py:35
  143.5 199.1 %all-gather.5.cloned.1.call-start = ((), (), s32[]{:S(2)}) async-start(), calls=%async_computation.5 | async-start | bytes 15728640 | tf_op jit(solution)/shard_map/all_gather | solution.py:54
  174.6 5.8 %copy-start.2 = (bf16[128,1024]{1,0:T(8,128)(2,1)}, bf16[128,1024]{1,0:T(8,128)(2,1)S(1)}, u32[]{:S(2)}) copy-start(bf16[128,1024]{1,0:T(8,128)(2,1)S(1)} %get-tuple-element.8) | copy-start | bytes 786436
  262.4 86.8 %slice-start = ((s8[6291456]{0:T(1024)(128)(4,1)}), s8[2097152]{0:T(1024)(128)(4,1)S(1)}, s32[]{:S(2)}) async-start(s8[6291456]{0:T(1024)(128)(4,1)} %bitcast.36), calls=%async_computation.6 | async-start | bytes 4194304
  342.7 6.6 %slice-start.1 = ((s8[6291456]{0:T(1024)(128)(4,1)}), s8[4194304]{0:T(1024)(128)(4,1)S(1)}, s32[]{:S(2)}) async-start(s8[6291456]{0:T(1024)(128)(4,1)} %bitcast.36), calls=%async_computation.7 | async-start | bytes 8388608
  366.6 27.8 %collective-permute-start.1 = (bf16[2,768,384]{2,1,0:T(8,128)(2,1)S(1)}, bf16[2,768,384]{2,1,0:T(8,128)(2,1)S(1)}, u32[]{:S(2)}, u32[]{:S(2)}) collective-permute-start(bf16[2,768,384]{2,1,0:T(8,128)(2,1)S(1)} %multiply_convert_fusion), channel_id=1, source_target_pairs={{0,1},{1,2},{2,3},{3,0},{4,5},{5,6},{6,7},{7,4},{8,9},{9,10},{10,1... | collective-permute-start | bytes 3538952 | tf_op jit(solution)/shard_map/ppermute | solution.py:82
  366.9 33.9 %collective-permute-start = (bf16[2,768,384]{2,1,0:T(8,128)(2,1)S(1)}, bf16[2,768,384]{2,1,0:T(8,128)(2,1)}, u32[]{:S(2)}, u32[]{:S(2)}) collective-permute-start(bf16[2,768,384]{2,1,0:T(8,128)(2,1)S(1)} %multiply_convert_fusion), channel_id=1, source_target_pairs={{0,3},{1,0},{2,1},{3,2},{4,7},{5,4},{6,5},{7,6},{8,11},{9,8},{10,9... | collective-permute-start | bytes 3538952 | tf_op jit(solution)/shard_map/ppermute | solution.py:84
  394.3 15.7 %collective-permute-start.2 = (bf16[2,768,384]{2,1,0:T(8,128)(2,1)S(1)}, bf16[2,768,384]{2,1,0:T(8,128)(2,1)}, u32[]{:S(2)}, u32[]{:S(2)}) collective-permute-start(bf16[2,768,384]{2,1,0:T(8,128)(2,1)S(1)} %collective-permute-done.1), channel_id=1, source_target_pairs={{0,1},{1,2},{2,3},{3,0},{4,5},{5,6},{6,7},{7,4},{8,9},{9,10},{10,1... | collective-permute-start | bytes 3538952 | tf_op jit(solution)/shard_map/ppermute | solution.py:82
  415.9 5.5 %copy-start.5 = (f32[128,8]{0,1:T(8,128)S(1)}, f32[128,8]{0,1:T(8,128)}, u32[]{:S(2)}) copy-start(f32[128,8]{0,1:T(8,128)} %param.17) | copy-start | bytes 12292
  415.9 73.3 %all-to-all-start.1 = ((bf16[8,2,96,1024]{3,2,1,0:T(8,128)(2,1)}), bf16[8,2,96,1024]{3,2,1,0:T(8,128)(2,1)S(1)}, u32[]{:S(2)}, u32[]{:S(2)}) async-start(bf16[8,2,96,1024]{3,2,1,0:T(8,128)(2,1)} %bitcast.31), calls=%async_computation.2 | async-start | bytes 6291456 | tf_op jit(solution)/shard_map/all_to_all | solution.py:99
  489.2 8.6 %copy-start.1 = (bf16[128,1024]{1,0:T(8,128)(2,1)S(1)}, bf16[128,1024]{1,0:T(8,128)(2,1)}, u32[]{:S(2)}) copy-start(bf16[128,1024]{1,0:T(8,128)(2,1)} %param.9) | copy-start | bytes 786436
  494.5 2.4 copy-start.3
Sparse Core Ops, SparseCore 0:
  9.4 128.0 all-gather.2
  143.7 29.5 reduce-scatter.1
  262.6 80.0 all-gather.4
